TPU v7x, 256 devices: a whole 4x4x8 slice. The times are simulated.
256 devices in a mesh: ctx: 32 (over y, z), tp: 8 (over x, core).
Axes of the slice: x: 4, y: 4, z: 8, core: 2. Of those that a mesh axis runs over, the one named last changes fastest.
Arguments:
- residual: bfloat16 [8192, 8192], P('ctx', 'tp'), may hold values from -90 to 90
- hyena_gate: bfloat16 [8192, 8192], P('ctx', 'tp'), may hold values from -6 to 6
- hyena_key: bfloat16 [8192, 8192], P('ctx', 'tp'), may hold values from -6 to 6
- hyena_value: bfloat16 [8192, 8192], P('ctx', 'tp'), may hold values from -6 to 6
- filter_taps: float32 [512, 128], P('tp'), may hold values from -0.45 to 0.45
- norm_gain: float32 [8192], P('tp'), may hold values from 0.5 to 1.5
- att_query: bfloat16 [8192, 8192], P('ctx', 'tp'), may hold values from -180 to 180
- att_key: bfloat16 [8192, 8192], P('ctx', 'tp'), may hold values from -6 to 6
- att_value: bfloat16 [8192, 8192], P('ctx', 'tp'), may hold values from -6 to 6
- doc_lengths: int32 [32], replicated, may hold values from 1 to 768, 8192 in all
Outputs:
- normed: bfloat16 [8192, 8192], P('ctx', 'tp')
- attended: bfloat16 [8192, 8192], P('ctx', 'tp')
Inputs may be any that keep to these rules, and one draw needn't show every extreme that they name: `doc_lengths`: the lengths sum to 8192; the longest document has exactly 768 tokens.
All inputs are finite; a program needn't handle non-finite values.
Results may differ from a plain program's by a relative error of at most 0.0075.
Values may be sent and summed in bfloat16 or wider, within the bound.
No kernel may reach another device: no remote copies, remote signals or barrier semaphores. Data moves between devices by JAX's collectives and lax.ppermute only.
A program may use at most 128 MiB of HBM per device.

v0:
```python
import jax
import jax.numpy as jnp
from jax import lax
from jax.sharding import PartitionSpec as P

D = 8192
HEAD_DIM = 128
REACH = 3
norm_epsilon = 1e-05


def shifted(value, axis, steps):
    count = lax.axis_size(axis)
    first, last = (max(0, -steps), min(count, count - steps))
    return lax.ppermute(value, axis, [(source, source + steps) for source in range(first, last)])


def document_begin(doc_lengths, positions):
    count = doc_lengths.shape[0]
    order = jnp.arange(count, dtype=jnp.int32)
    before = order[None, :] < order[:, None]
    starts = jnp.sum(jnp.where(before, doc_lengths[None, :], 0), axis=1)
    return jnp.max(jnp.where(starts[None, :] <= positions[:, None], starts[None, :], 0), axis=1)


def causal_filter(extended, filter_taps, reach_back, out_rows):
    groups, taps = filter_taps.shape
    channels = extended.shape[1]
    width = channels // groups
    lag_table = (
        jnp.arange(taps, dtype=jnp.int32)[:, None]
        + (taps - 1)
        - jnp.arange(2 * taps - 1, dtype=jnp.int32)[None, :]
    )
    reversed_taps = filter_taps[:, ::-1]
    period = jnp.concatenate([reversed_taps, jnp.zeros((groups, taps), jnp.float32)], axis=1)
    tiled = jnp.tile(period, (1, taps))
    toeplitz = tiled[:, : taps * (2 * taps - 1)].reshape(groups, taps, 2 * taps - 1)
    upper_part = toeplitz.astype(jnp.bfloat16)
    lower_part = (toeplitz - upper_part.astype(jnp.float32)).astype(jnp.bfloat16)
    zero_half = jnp.zeros((), jnp.bfloat16)
    numbers = (((0,), (2,)), ((1,), (0,)))
    results = []
    for block_index in range(out_rows // taps):
        first = block_index * taps
        sources = extended[first : first + 2 * taps - 1].reshape(2 * taps - 1, groups, width)
        limits = reach_back[first : first + taps]
        valid = (lag_table <= limits[:, None])[None]
        kernel_upper = jnp.where(valid, upper_part, zero_half)
        kernel_lower = jnp.where(valid, lower_part, zero_half)
        result = lax.dot_general(sources, kernel_upper, numbers, preferred_element_type=jnp.float32)
        result = result + lax.dot_general(
            sources, kernel_lower, numbers, preferred_element_type=jnp.float32
        )
        results.append(result.transpose(2, 0, 1).reshape(taps, channels))
    return jnp.concatenate(results, axis=0)


def attend_part(query_head, key_head, value_head, visible, scale):
    scores = (
        lax.dot_general(
            query_head, key_head, (((1,), (1,)), ((), ())), preferred_element_type=jnp.float32
        )
        * scale
    )
    scores = jnp.where(visible, scores, jnp.float32(-1e30))
    top = jnp.max(scores, axis=1, keepdims=True)
    expo = jnp.where(visible, jnp.exp(scores - top), jnp.float32(0.0))
    denominator = jnp.sum(expo, axis=1, keepdims=True)
    summed = jnp.dot(expo.astype(jnp.bfloat16), value_head, preferred_element_type=jnp.float32)
    return (summed, top, denominator)


def attend_block(queries, keys, values, visible, scale):
    head_count = queries.shape[1] // HEAD_DIM
    sums, tops, dens = ([], [], [])
    for head_index in range(head_count):
        lower = head_index * HEAD_DIM
        upper = lower + HEAD_DIM
        summed, top, den = attend_part(
            queries[:, lower:upper], keys[:, lower:upper], values[:, lower:upper], visible, scale
        )
        sums.append(summed)
        tops.append(top)
        dens.append(den)
    return (jnp.stack(sums, axis=1), jnp.concatenate(tops, axis=1), jnp.concatenate(dens, axis=1))


def on_device(
    residual,
    hyena_gate,
    hyena_key,
    hyena_value,
    filter_taps,
    norm_gain,
    att_query,
    att_key,
    att_value,
    doc_lengths,
):
    tok_rows = residual.shape[0]
    taps = filter_taps.shape[1]
    shard_index = lax.axis_index("ctx")
    anchor = shard_index * tok_rows
    positions = anchor + jnp.arange(tok_rows, dtype=jnp.int32)
    doc_begin = document_begin(doc_lengths, positions)
    mixed_rows = (hyena_key.astype(jnp.float32) * hyena_value.astype(jnp.float32)).astype(
        jnp.bfloat16
    )
    rim_rows = shifted(mixed_rows[tok_rows - (taps - 1) :], "ctx", 1)
    key_pair = jnp.stack([att_key, att_value])
    previous = shifted(key_pair, "ctx", 1)
    later_query = shifted(att_query, "ctx", -2)
    key_rows = jnp.concatenate([previous[0], att_key], axis=0)
    value_rows = jnp.concatenate([previous[1], att_value], axis=0)
    window = key_rows.shape[0]
    key_pos = anchor - tok_rows + jnp.arange(window, dtype=jnp.int32)
    scale = jnp.float32(1.0 / HEAD_DIM**0.5)
    far_pos = positions + 2 * tok_rows
    far_begin = document_begin(doc_lengths, far_pos)
    far_visible = (key_pos[None, :] <= far_pos[:, None]) & (key_pos[None, :] >= far_begin[:, None])
    far_sum, far_top, far_den = attend_block(later_query, key_rows, value_rows, far_visible, scale)
    far_packet = (far_sum.astype(jnp.bfloat16), far_top, far_den)
    far_packet, mixed_rows = lax.optimization_barrier((far_packet, mixed_rows))
    far_sum, far_top, far_den = shifted(far_packet, "ctx", 2)
    extended = jnp.concatenate([rim_rows, mixed_rows], axis=0)
    filtered = causal_filter(extended, filter_taps, positions - doc_begin, tok_rows)
    hidden = residual.astype(jnp.float32) + hyena_gate.astype(jnp.float32) * filtered
    local_sum = jnp.sum(hidden * hidden, axis=1)
    mean_square = lax.psum(local_sum, "tp") / D
    normed = (hidden * lax.rsqrt(mean_square + norm_epsilon)[:, None] * norm_gain[None, :]).astype(
        jnp.bfloat16
    )
    visible = (key_pos[None, :] <= positions[:, None]) & (key_pos[None, :] >= doc_begin[:, None])
    near_sum, near_top, near_den = attend_block(att_query, key_rows, value_rows, visible, scale)
    far_top = jnp.where(far_den > 0, far_top, jnp.float32(-1e30))
    top = jnp.maximum(near_top, far_top)
    near_scale = jnp.exp(near_top - top)
    far_scale = jnp.exp(far_top - top)
    denominator = near_den * near_scale + far_den * far_scale
    summed = near_sum * near_scale[:, :, None] + far_sum.astype(jnp.float32) * far_scale[:, :, None]
    attended = (summed / denominator[:, :, None]).astype(jnp.bfloat16).reshape(tok_rows, -1)
    return (normed, attended)


def solution(mesh):
    placed = (
        P("ctx", "tp"),
        P("ctx", "tp"),
        P("ctx", "tp"),
        P("ctx", "tp"),
        P("tp", None),
        P("tp"),
        P("ctx", "tp"),
        P("ctx", "tp"),
        P("ctx", "tp"),
        P(),
    )
    return jax.shard_map(
        on_device,
        mesh=mesh,
        in_specs=placed,
        out_specs=(P("ctx", "tp"), P("ctx", "tp")),
        check_vma=False,
    )
```

profile of v0, /device:TPU:32, one launch (start us, length us, event | category | flops | bytes accessed | tf_op | source)
XLA Modules:
  0.0 137.4 jit_solution(9986038495159426855)
XLA Ops:
  0.6 1.4 %multiply_convert_fusion.1 = bf16[256,1024]{1,0:T(8,128)(2,1)S(1)} fusion(bf16[256,1024]{1,0:T(8,128)(2,1)} %param.13, bf16[256,1024]{1,0:T(8,128)(2,1)} %param.12), kind=kLoop, calls=%fused_computation.141 | loop fusion | flops 1048576 | bytes 1572864 | tf_op jit(solution)/shard_map/convert_element_type | solution.py:107
  2.8 3.8 %collective-permute-start = (bf16[127,1024]{1,0:T(8,128)(2,1)}, bf16[127,1024]{1,0:T(8,128)(2,1)S(1)}, u32[]{:S(2)}, u32[]{:S(2)}) collective-permute-start(bf16[127,1024]{1,0:T(8,128)(2,1)} %slice.176), channel_id=1, source_target_pairs={{0,8},{8,16},{16,24},{24,32},{32,40},{40,48},{48,56},{56,64},{64,7... | collective-permute-start | bytes 780296 | tf_op jit(solution)/shard_map/ppermute | solution.py:15
  6.6 1.3 collective-permute-start.2
  7.9 2.3 %pad_maximum_fusion = bf16[2,256,1024]{2,1,0:T(8,128)(2,1)} fusion(bf16[1,256,1024]{2,1,0:T(8,128)(2,1)} %bitcast.185, bf16[1,256,1024]{2,1,0:T(8,128)(2,1)} %bitcast.186), kind=kLoop, calls=%fused_computation.135 | loop fusion | flops 524288 | bytes 2097152 | tf_op jit(solution)/shard_map/stack | solution.py:111
  10.2 4.4 %collective-permute-start.1 = (bf16[2,256,1024]{2,1,0:T(8,128)(2,1)}, bf16[2,256,1024]{2,1,0:T(8,128)(2,1)S(1)}, u32[]{:S(2)}, u32[]{:S(2)}) collective-permute-start(bf16[2,256,1024]{2,1,0:T(8,128)(2,1)} %pad_maximum_fusion), channel_id=1, source_target_pairs={{0,8},{8,16},{16,24},{24,32},{32,40},{40,48},{48,56},{56,64},{64,7... | collective-permute-start | bytes 3145736 | tf_op jit(solution)/shard_map/ppermute | solution.py:15
  15.5 4.7 %copy.60 = f32[8,8,128,256]{3,1,2,0:T(8,128)S(1)} copy(f32[8,8,128,256]{3,2,1,0:T(8,128)S(1)} %bitcast.187) | data formatting | bytes 16777216
  20.2 3.7 %slice.215 = f32[64,32640]{1,0:T(8,128)} slice(f32[64,32768]{1,0:T(8,128)S(1)} %bitcast.188), slice={[0:64], [0:32640]} | slice | bytes 16711680 | tf_op jit(solution)/shard_map/slice | solution.py:38
  24.0 16.0 %reshape.128 = f32[64,128,255]{2,1,0:T(8,128)} reshape(f32[64,32640]{1,0:T(8,128)} %slice.215) | data formatting | bytes 16711680 | tf_op jit(solution)/shard_map/reshape | solution.py:38
  40.4 1.2 fusion.262
  41.6 1.1 fusion.256
  43.9 1.1 fusion.258
  47.2 1.1 fusion.248
  50.3 1.1 fusion.250
  51.8 1.1 fusion.251
  53.4 1.1 fusion.252
  54.9 1.1 fusion.253
  56.5 1.1 fusion.254
  59.2 1.4 fusion.93
  63.4 6.0 %collective-permute-start.3 = (f32[256,8]{0,1:T(8,128)S(1)}, f32[256,8]{0,1:T(8,128)S(1)}, u32[]{:S(2)}, u32[]{:S(2)}) collective-permute-start(f32[256,8]{0,1:T(8,128)S(1)} %concatenate.30), channel_id=1, source_target_pairs={{0,16},{8,24},{16,32},{24,40},{32,48},{40,56},{48,64},{56,72},{64,... | collective-permute-start | bytes 24584 | tf_op jit(solution)/shard_map/ppermute | solution.py:15
  69.4 4.5 %collective-permute-start.4 = (f32[256,8]{0,1:T(8,128)}, f32[256,8]{0,1:T(8,128)S(1)}, u32[]{:S(2)}, u32[]{:S(2)}) collective-permute-start(f32[256,8]{0,1:T(8,128)} %concatenate.29), channel_id=1, source_target_pairs={{0,16},{8,24},{16,32},{24,40},{32,48},{40,56},{48,64},{56,72},{64,... | collective-permute-start | bytes 24584 | tf_op jit(solution)/shard_map/ppermute | solution.py:15
  73.9 2.0 %fusion.263 = (f32[256]{0:T(256)S(1)}, f32[256,512]{0,1:T(8,128)}) fusion(bf16[512,128]{1,0:T(8,128)(2,1)} %copy-done.12, bf16[256,1024]{1,0:T(8,128)(2,1)} %param.16, s32[256]{0:T(256)S(1)} %get-tuple-element.30, s32[256]{0:T(256)S(1)} %iota_add_fusion.1, s32[512]{0:T(512)S(1)} %iota_add_fusion), kind=kOutput, calls=%fused_computation.316 | convolution fusion | flops 34340608 | bytes 726016 | tf_op jit(solution)/shard_map/dot_general | solution.py:61
  77.1 1.2 copy.39
  78.3 6.1 %collective-permute-start.5 = (bf16[256,8,128]{2,0,1:T(8,128)(2,1)}, bf16[256,8,128]{2,0,1:T(8,128)(2,1)}, u32[]{:S(2)}, u32[]{:S(2)}) collective-permute-start(bf16[256,8,128]{2,0,1:T(8,128)(2,1)} %copy-done.14), channel_id=1, source_target_pairs={{0,16},{8,24},{16,32},{24,40},{32,48},{40,56},{48,64},{56,72},{64,... | collective-permute-start | bytes 1572872 | tf_op jit(solution)/shard_map/ppermute | solution.py:15
  84.4 7.0 %fusion = f32[64,16,128]{2,1,0:T(8,128)S(1)} fusion(bf16[255,64,16]{0,2,1:T(8,128)(2,1)S(1)} %bitcast.191, pred[128,255]{1,0:T(8,128)(4,1)S(1)} %get-tuple-element.42, f32[64,128,255]{2,1,0:T(8,128)} %reshape.128), kind=kOutput, calls=%fused_computation.1 | convolution fusion | flops 77291520 | bytes 9435008 | tf_op jit(solution)/shard_map/dot_general | solution.py:52
  91.4 5.4 %fusion.51 = f32[64,16,128]{2,1,0:T(8,128)} fusion(f32[64,16,128]{2,1,0:T(8,128)S(1)} %fusion, bf16[255,64,16]{0,2,1:T(8,128)(2,1)S(1)} %bitcast.192, pred[128,255]{1,0:T(8,128)(4,1)S(1)} %get-tuple-element.42, f32[64,128,255]{2,1,0:T(8,128)} %reshape.128), kind=kOutput, calls=%fused_computation.94 | convolution fusion | flops 71155712 | bytes 9959296 | tf_op jit(solution)/shard_map/dot_general | solution.py:51
  96.8 2.1 %copy.41 = f32[128,1024]{1,0:T(8,128)} copy(f32[128,1024]{0,1:T(8,128)} %bitcast.194) | data formatting | bytes 1048576 | tf_op jit(solution)/shard_map/reshape | solution.py:55
  98.8 7.0 %fusion.4 = f32[64,16,128]{2,1,0:T(8,128)S(1)} fusion(bf16[255,64,16]{0,2,1:T(8,128)(2,1)S(1)} %bitcast.189, pred[128,255]{1,0:T(8,128)(4,1)S(1)} %get-tuple-element.41, f32[64,128,255]{2,1,0:T(8,128)} %reshape.128), kind=kOutput, calls=%fused_computation.5 | convolution fusion | flops 77291520 | bytes 9435008 | tf_op jit(solution)/shard_map/dot_general | solution.py:52
  105.8 4.6 %fusion.48 = f32[64,16,128]{2,1,0:T(8,128)S(1)} fusion(f32[64,16,128]{2,1,0:T(8,128)S(1)} %fusion.4, bf16[255,64,16]{0,2,1:T(8,128)(2,1)S(1)} %bitcast.190, pred[128,255]{1,0:T(8,128)(4,1)S(1)} %get-tuple-element.41, f32[64,128,255]{2,1,0:T(8,128)} %reshape.128), kind=kOutput, calls=%fused_computation.93 | convolution fusion | flops 71155712 | bytes 9959296 | tf_op jit(solution)/shard_map/dot_general | solution.py:51
  111.4 1.9 %multiply_reduce_fusion = f32[256]{0:T(256)S(1)} fusion(f32[128,1024]{1,0:T(8,128)} %copy.41, f32[128,1024]{1,0:T(8,128)} %copy.40, bf16[256,1024]{1,0:T(8,128)(2,1)} %param.11, bf16[256,1024]{1,0:T(8,128)(2,1)} %param.10), kind=kLoop, calls=%fused_computation.140 | loop fusion | flops 1834752 | bytes 2098176 | tf_op jit(solution)/shard_map/reduce_sum | solution.py:129
  113.2 12.9 %psum.7 = f32[256]{0:T(256)S(1)} all-reduce(f32[256]{0:T(256)S(1)} %multiply_reduce_fusion), channel_id=1, replica_groups=mesh['ctx'=32,'tp'=8] {'tp'}, use_global_device_ids=true, to_apply=%region_20.21 | all-reduce | flops 256 | bytes 2048 | tf_op jit(solution)/shard_map/psum | solution.py:130
  126.6 2.6 %multiply_convert_fusion = bf16[256,1024]{1,0:T(8,128)(2,1)} fusion(f32[1024]{0:T(1024)S(1)} %copy-done.15, f32[256]{0:T(256)S(1)} %add_rsqrt_fusion, f32[128,1024]{1,0:T(8,128)} %copy.41, f32[128,1024]{1,0:T(8,128)} %copy.40, bf16[256,1024]{1,0:T(8,128)(2,1)} %param.11, bf16[256,1024]{1,0:T(8,128)(2,1)} %param.10), kind=kLoop, calls=%fused_computation.139 | loop fusion | flops 2097152 | bytes 2626560 | tf_op jit(solution)/shard_map/convert_element_type | solution.py:131
  134.1 2.1 %divide_convert_fusion = bf16[256,8,128]{2,0,1:T(8,128)(2,1)S(1)} fusion(bf16[256,8,128]{2,0,1:T(8,128)(2,1)} %collective-permute-done.5, f32[256,8,128]{2,0,1:T(8,128)} %copy-done.7, f32[256,8]{0,1:T(8,128)S(1)} %get-tuple-element.32, f32[256,8]{0,1:T(8,128)S(1)} %get-tuple-element.34, f32[256,8]{0,1:T(8,128)S(1)} %get-tuple-element.33), kind=kLoop, calls=%fused_computation.138 | loop fusion | flops 1572864 | bytes 2121728 | tf_op jit(solution)/shard_map/convert_element_type | solution.py:142
  (88 shorter events, 21.8 us)
Async XLA Ops:
  0.6 14.1 %copy-start.13 = (f32[64,128]{1,0:T(8,128)S(1)}, f32[64,128]{1,0:T(8,128)}, u32[]{:S(2)}) copy-start(f32[64,128]{1,0:T(8,128)} %param.14) | copy-start | bytes 98308
  2.8 73.1 %collective-permute-start = (bf16[127,1024]{1,0:T(8,128)(2,1)}, bf16[127,1024]{1,0:T(8,128)(2,1)S(1)}, u32[]{:S(2)}, u32[]{:S(2)}) collective-permute-start(bf16[127,1024]{1,0:T(8,128)(2,1)} %slice.176), channel_id=1, source_target_pairs={{0,8},{8,16},{16,24},{24,32},{32,40},{40,48},{48,56},{56,64},{64,7... | collective-permute-start | bytes 780296 | tf_op jit(solution)/shard_map/ppermute | solution.py:15
  6.6 40.6 %collective-permute-start.2 = (bf16[256,1024]{1,0:T(8,128)(2,1)}, bf16[256,1024]{1,0:T(8,128)(2,1)}, u32[]{:S(2)}, u32[]{:S(2)}) collective-permute-start(bf16[256,1024]{1,0:T(8,128)(2,1)} %param.16), channel_id=1, source_target_pairs={{16,0},{24,8},{32,16},{40,24},{48,32},{56,40},{64,48},{72,56},{80,... | collective-permute-start | bytes 1572872 | tf_op jit(solution)/shard_map/ppermute | solution.py:15
  10.2 30.1 %collective-permute-start.1 = (bf16[2,256,1024]{2,1,0:T(8,128)(2,1)}, bf16[2,256,1024]{2,1,0:T(8,128)(2,1)S(1)}, u32[]{:S(2)}, u32[]{:S(2)}) collective-permute-start(bf16[2,256,1024]{2,1,0:T(8,128)(2,1)} %pad_maximum_fusion), channel_id=1, source_target_pairs={{0,8},{8,16},{16,24},{24,32},{32,40},{40,48},{48,56},{56,64},{64,7... | collective-permute-start | bytes 3145736 | tf_op jit(solution)/shard_map/ppermute | solution.py:15
  24.0 16.0 %copy-start.16 = (s32[32]{0:T(128)S(1)}, s32[32]{0:T(128)}, u32[]{:S(2)}) copy-start(s32[32]{0:T(128)} %param.19) | copy-start | bytes 388
  24.0 16.5 %copy-start.1 = (bf16[256,1024]{1,0:T(8,128)(2,1)S(1)}, bf16[256,1024]{1,0:T(8,128)(2,1)}, u32[]{:S(2)}) copy-start(bf16[256,1024]{1,0:T(8,128)(2,1)} %param.17) | copy-start | bytes 1572868
  40.0 2.8 %copy-start.9 = (bf16[256,1024]{1,0:T(8,128)(2,1)S(1)}, bf16[256,1024]{1,0:T(8,128)(2,1)}, u32[]{:S(2)}) copy-start(bf16[256,1024]{1,0:T(8,128)(2,1)} %param.16) | copy-start | bytes 1572868
  40.3 4.7 %copy-start = (bf16[256,1024]{1,0:T(8,128)(2,1)S(1)}, bf16[256,1024]{1,0:T(8,128)(2,1)}, u32[]{:S(2)}) copy-start(bf16[256,1024]{1,0:T(8,128)(2,1)} %param.18) | copy-start | bytes 1572868
  45.1 13.0 %copy-start.12 = (bf16[512,128]{1,0:T(8,128)(2,1)}, bf16[512,128]{1,0:T(8,128)(2,1)S(1)}, u32[]{:S(2)}) copy-start(bf16[512,128]{1,0:T(8,128)(2,1)S(1)} %get-tuple-element.76) | copy-start | bytes 393220
  45.1 15.5 %copy-start.10 = (bf16[512,128]{1,0:T(8,128)(2,1)}, bf16[512,128]{1,0:T(8,128)(2,1)S(1)}, u32[]{:S(2)}) copy-start(bf16[512,128]{1,0:T(8,128)(2,1)S(1)} %get-tuple-element.75) | copy-start | bytes 393220
  61.0 1.1 copy-start.14
  63.4 70.6 %collective-permute-start.3 = (f32[256,8]{0,1:T(8,128)S(1)}, f32[256,8]{0,1:T(8,128)S(1)}, u32[]{:S(2)}, u32[]{:S(2)}) collective-permute-start(f32[256,8]{0,1:T(8,128)S(1)} %concatenate.30), channel_id=1, source_target_pairs={{0,16},{8,24},{16,32},{24,40},{32,48},{40,56},{48,64},{56,72},{64,... | collective-permute-start | bytes 24584 | tf_op jit(solution)/shard_map/ppermute | solution.py:15
  69.4 64.6 %collective-permute-start.4 = (f32[256,8]{0,1:T(8,128)}, f32[256,8]{0,1:T(8,128)S(1)}, u32[]{:S(2)}, u32[]{:S(2)}) collective-permute-start(f32[256,8]{0,1:T(8,128)} %concatenate.29), channel_id=1, source_target_pairs={{0,16},{8,24},{16,32},{24,40},{32,48},{40,56},{48,64},{56,72},{64,... | collective-permute-start | bytes 24584 | tf_op jit(solution)/shard_map/ppermute | solution.py:15
  78.3 55.7 %collective-permute-start.5 = (bf16[256,8,128]{2,0,1:T(8,128)(2,1)}, bf16[256,8,128]{2,0,1:T(8,128)(2,1)}, u32[]{:S(2)}, u32[]{:S(2)}) collective-permute-start(bf16[256,8,128]{2,0,1:T(8,128)(2,1)} %copy-done.14), channel_id=1, source_target_pairs={{0,16},{8,24},{16,32},{24,40},{32,48},{40,56},{48,64},{56,72},{64,... | collective-permute-start | bytes 1572872 | tf_op jit(solution)/shard_map/ppermute | solution.py:15
  110.4 16.2 %copy-start.15 = (f32[1024]{0:T(1024)S(1)}, f32[1024]{0:T(1024)}, u32[]{:S(2)}) copy-start(f32[1024]{0:T(1024)} %param.15) | copy-start | bytes 12292
  110.4 18.8 %copy-start.2 = (f32[256,512]{0,1:T(8,128)S(1)}, f32[256,512]{0,1:T(8,128)}, u32[]{:S(2)}) copy-start(f32[256,512]{0,1:T(8,128)} %get-tuple-element.62) | copy-start | bytes 1572868
  111.4 18.2 %copy-start.3 = (f32[256,512]{0,1:T(8,128)S(1)}, f32[256,512]{0,1:T(8,128)}, u32[]{:S(2)}) copy-start(f32[256,512]{0,1:T(8,128)} %get-tuple-element.64) | copy-start | bytes 1572868
  126.2 3.9 %copy-start.4 = (f32[256,512]{0,1:T(8,128)S(1)}, f32[256,512]{0,1:T(8,128)}, u32[]{:S(2)}) copy-start(f32[256,512]{0,1:T(8,128)} %get-tuple-element.66) | copy-start | bytes 1572868
  126.6 3.9 %copy-start.5 = (f32[256,512]{0,1:T(8,128)S(1)}, f32[256,512]{0,1:T(8,128)}, u32[]{:S(2)}) copy-start(f32[256,512]{0,1:T(8,128)} %get-tuple-element.68) | copy-start | bytes 1572868
  126.6 4.3 %copy-start.6 = (f32[256,512]{0,1:T(8,128)S(1)}, f32[256,512]{0,1:T(8,128)}, u32[]{:S(2)}) copy-start(f32[256,512]{0,1:T(8,128)} %get-tuple-element.70) | copy-start | bytes 1572868
  129.2 2.1 %copy-start.8 = (f32[256,512]{0,1:T(8,128)S(1)}, f32[256,512]{0,1:T(8,128)}, u32[]{:S(2)}) copy-start(f32[256,512]{0,1:T(8,128)} %get-tuple-element.74) | copy-start | bytes 1572868
  130.9 1.7 %copy-start.11 = (bf16[512,128]{1,0:T(8,128)(2,1)S(1)}, bf16[512,128]{1,0:T(8,128)(2,1)}, u32[]{:S(2)}) copy-start(bf16[512,128]{1,0:T(8,128)(2,1)} %copy-done.10) | copy-start | bytes 393220
  133.0 1.0 copy-start.7
where the time goes:
time: 138 us; the launch traced here: 137 us
  matrix products  49.2 us (36%)
  local copies, waits for them, and re-layouts  34.2 us (25%)
  starting transfers between devices  26.1 us (19%)
  other arithmetic  13.9 us (10%)
  blocking collectives  12.9 us (9%)
    ppermute x6, starting transfers between devices, shifted(): lax.ppermute(value, axis, [(source, source + steps) for source in range(f...  26.1 us
    dot_general x16, matrix products, attend_part(): lax.dot_general(query_head, key_head, (((1,), (1,)), ((), ())), preferred...  18.7 us
    reshape x1, local copies, waits for them, and re-layouts, causal_filter(): tiled[:, :taps * (2 * taps - 1)].reshape(groups, taps, 2 * taps - 1)  16 us
    dot_general x2, matrix products, causal_filter(): lax.dot_general(sources, kernel_lower, numbers, preferred_element_type=jn...  13.9 us
    psum x1, blocking collectives, on_device(): mean_square = lax.psum(local_sum, 'tp') / D  12.9 us
    dot_general x2, matrix products, causal_filter(): lax.dot_general(sources, kernel_upper, numbers, preferred_element_type=jn...  9.99 us
    unnamed x36, local copies, waits for them, and re-layouts  6.79 us
    dot_general x16, matrix products, attend_part(): jnp.dot(expo.astype(jnp.bfloat16), value_head, preferred_element_type=jnp...  6.62 us
  transfers between devices with their start and end apart: 6, of which 0 were waited for; matrix products, arithmetic and copies ran while one was open for 66% of the time, Pallas kernels for 0%

commit v1 on v0

--- a/solution.py
+++ b/solution.py
@@ -127,7 +127,7 @@
     filtered = causal_filter(extended, filter_taps, positions - doc_begin, tok_rows)
     hidden = residual.astype(jnp.float32) + hyena_gate.astype(jnp.float32) * filtered
     local_sum = jnp.sum(hidden * hidden, axis=1)
-    mean_square = lax.psum(local_sum, "tp") / D
+    mean_square = jnp.sum(lax.all_gather(local_sum, "tp"), axis=0) / D
     normed = (hidden * lax.rsqrt(mean_square + norm_epsilon)[:, None] * norm_gain[None, :]).astype(
         jnp.bfloat16
     )

time: 138 us -> 137 us (level)
  blocking collectives: 12.9 us -> 10.6 us
    psum x1 -> x0, blocking collectives: 12.9 us -> none  [on_device(): mean_square = lax.psum(local_sum, 'tp') / D]
    all_gather x0 -> x1, blocking collectives: none -> 10.6 us  [on_device(): mean_square = jnp.sum(lax.all_gather(local_sum, 'tp'), axis=0) / D]
  transfers between devices with their start and end apart: 6 -> 6, of which waited for: 0 -> 0; matrix products, arithmetic and copies ran while one was open for 66% -> 67% of each run, Pallas kernels for 0% -> 0%
where the time goes in v1:
time: 137 us; the launch traced here: 135 us
  matrix products  49.2 us (36%)
  local copies, waits for them, and re-layouts  34.2 us (25%)
  starting transfers between devices  26.1 us (19%)
  other arithmetic  13.9 us (10%)
  blocking collectives  10.6 us (8%)
    ppermute x6, starting transfers between devices, shifted(): lax.ppermute(value, axis, [(source, source + steps) for source in range(f...  26.1 us
    dot_general x16, matrix products, attend_part(): lax.dot_general(query_head, key_head, (((1,), (1,)), ((), ())), preferred...  18.7 us
    reshape x1, local copies, waits for them, and re-layouts, causal_filter(): tiled[:, :taps * (2 * taps - 1)].reshape(groups, taps, 2 * taps - 1)  16 us
    dot_general x2, matrix products, causal_filter(): lax.dot_general(sources, kernel_lower, numbers, preferred_element_type=jn...  13.9 us
    all_gather x1, blocking collectives, on_device(): mean_square = jnp.sum(lax.all_gather(local_sum, 'tp'), axis=0) / D  10.6 us
    dot_general x2, matrix products, causal_filter(): lax.dot_general(sources, kernel_upper, numbers, preferred_element_type=jn...  9.99 us
    unnamed x36, local copies, waits for them, and re-layouts  6.79 us
    dot_general x16, matrix products, attend_part(): jnp.dot(expo.astype(jnp.bfloat16), value_head, preferred_element_type=jnp...  6.63 us
  transfers between devices with their start and end apart: 6, of which 0 were waited for; matrix products, arithmetic and copies ran while one was open for 67% of the time, Pallas kernels for 0%

profile of v1, /device:TPU:32, one launch (start us, length us, event | category | flops | bytes accessed | tf_op | source)
XLA Modules:
  0.0 135.1 jit_solution(8808588355087050539)
XLA Ops:
  0.6 1.4 %multiply_convert_fusion.1 = bf16[256,1024]{1,0:T(8,128)(2,1)S(1)} fusion(bf16[256,1024]{1,0:T(8,128)(2,1)} %param.13, bf16[256,1024]{1,0:T(8,128)(2,1)} %param.12), kind=kLoop, calls=%fused_computation.141 | loop fusion | flops 1048576 | bytes 1572864 | tf_op jit(solution)/shard_map/convert_element_type | solution.py:107
  2.8 3.8 %collective-permute-start = (bf16[127,1024]{1,0:T(8,128)(2,1)}, bf16[127,1024]{1,0:T(8,128)(2,1)S(1)}, u32[]{:S(2)}, u32[]{:S(2)}) collective-permute-start(bf16[127,1024]{1,0:T(8,128)(2,1)} %slice.176), channel_id=1, source_target_pairs={{0,8},{8,16},{16,24},{24,32},{32,40},{40,48},{48,56},{56,64},{64,7... | collective-permute-start | bytes 780296 | tf_op jit(solution)/shard_map/ppermute | solution.py:15
  6.6 1.3 collective-permute-start.2
  7.9 2.3 %pad_maximum_fusion = bf16[2,256,1024]{2,1,0:T(8,128)(2,1)} fusion(bf16[1,256,1024]{2,1,0:T(8,128)(2,1)} %bitcast.186, bf16[1,256,1024]{2,1,0:T(8,128)(2,1)} %bitcast.187), kind=kLoop, calls=%fused_computation.135 | loop fusion | flops 524288 | bytes 2097152 | tf_op jit(solution)/shard_map/stack | solution.py:111
  10.2 4.4 %collective-permute-start.1 = (bf16[2,256,1024]{2,1,0:T(8,128)(2,1)}, bf16[2,256,1024]{2,1,0:T(8,128)(2,1)S(1)}, u32[]{:S(2)}, u32[]{:S(2)}) collective-permute-start(bf16[2,256,1024]{2,1,0:T(8,128)(2,1)} %pad_maximum_fusion), channel_id=1, source_target_pairs={{0,8},{8,16},{16,24},{24,32},{32,40},{40,48},{48,56},{56,64},{64,7... | collective-permute-start | bytes 3145736 | tf_op jit(solution)/shard_map/ppermute | solution.py:15
  15.5 4.7 %copy.74 = f32[8,8,128,256]{3,1,2,0:T(8,128)S(1)} copy(f32[8,8,128,256]{3,2,1,0:T(8,128)S(1)} %bitcast.188) | data formatting | bytes 16777216
  20.2 3.7 %slice.215 = f32[64,32640]{1,0:T(8,128)} slice(f32[64,32768]{1,0:T(8,128)S(1)} %bitcast.189), slice={[0:64], [0:32640]} | slice | bytes 16711680 | tf_op jit(solution)/shard_map/slice | solution.py:38
  24.0 16.0 %reshape.132 = f32[64,128,255]{2,1,0:T(8,128)} reshape(f32[64,32640]{1,0:T(8,128)} %slice.215) | data formatting | bytes 16711680 | tf_op jit(solution)/shard_map/reshape | solution.py:38
  40.4 1.2 fusion.262
  41.6 1.1 fusion.256
  43.9 1.1 fusion.258
  47.2 1.1 fusion.248
  50.3 1.1 fusion.250
  51.8 1.1 fusion.251
  53.4 1.1 fusion.252
  54.9 1.1 fusion.253
  56.5 1.1 fusion.254
  59.2 1.4 %fusion.93 = (f32[256]{0:T(256)}, f32[256]{0:T(256)}, f32[256]{0:T(256)}, f32[256]{0:T(256)}, f32[256]{0:T(256)}, /*index=5*/f32[256]{0:T(256)}, f32[256]{0:T(256)}, f32[256]{0:T(256)}) fusion(f32[256,512]{0,1:T(8,128)S(1)} %get-tuple-element.60, f32[256]{0:T(256)S(1)} %get-tuple-element.59, s32[256]{0:T(256)S(1)} %get-tuple-element.33, ...), kind=kLoop, calls=%fused_computation.177 | loop fusion | flops 3536896 | bytes 4214784 | tf_op jit(solution)/shard_map/reduce_sum | solution.py:69
  63.4 6.0 %collective-permute-start.3 = (f32[256,8]{0,1:T(8,128)S(1)}, f32[256,8]{0,1:T(8,128)S(1)}, u32[]{:S(2)}, u32[]{:S(2)}) collective-permute-start(f32[256,8]{0,1:T(8,128)S(1)} %concatenate.30), channel_id=1, source_target_pairs={{0,16},{8,24},{16,32},{24,40},{32,48},{40,56},{48,64},{56,72},{64,... | collective-permute-start | bytes 24584 | tf_op jit(solution)/shard_map/ppermute | solution.py:15
  69.4 4.5 %collective-permute-start.4 = (f32[256,8]{0,1:T(8,128)}, f32[256,8]{0,1:T(8,128)S(1)}, u32[]{:S(2)}, u32[]{:S(2)}) collective-permute-start(f32[256,8]{0,1:T(8,128)} %concatenate.29), channel_id=1, source_target_pairs={{0,16},{8,24},{16,32},{24,40},{32,48},{40,56},{48,64},{56,72},{64,... | collective-permute-start | bytes 24584 | tf_op jit(solution)/shard_map/ppermute | solution.py:15
  73.9 2.0 %fusion.263 = (f32[256]{0:T(256)S(1)}, f32[256,512]{0,1:T(8,128)}) fusion(bf16[512,128]{1,0:T(8,128)(2,1)} %copy-done.12, bf16[256,1024]{1,0:T(8,128)(2,1)} %param.16, s32[256]{0:T(256)S(1)} %get-tuple-element.32, s32[256]{0:T(256)S(1)} %iota_add_fusion.1, s32[512]{0:T(512)S(1)} %iota_add_fusion), kind=kOutput, calls=%fused_computation.316 | convolution fusion | flops 34340608 | bytes 726016 | tf_op jit(solution)/shard_map/dot_general | solution.py:61
  77.1 1.2 copy.53
  78.3 6.1 %collective-permute-start.5 = (bf16[256,8,128]{2,0,1:T(8,128)(2,1)}, bf16[256,8,128]{2,0,1:T(8,128)(2,1)}, u32[]{:S(2)}, u32[]{:S(2)}) collective-permute-start(bf16[256,8,128]{2,0,1:T(8,128)(2,1)} %copy-done.14), channel_id=1, source_target_pairs={{0,16},{8,24},{16,32},{24,40},{32,48},{40,56},{48,64},{56,72},{64,... | collective-permute-start | bytes 1572872 | tf_op jit(solution)/shard_map/ppermute | solution.py:15
  84.4 7.0 %fusion = f32[64,16,128]{2,1,0:T(8,128)S(1)} fusion(bf16[255,64,16]{0,2,1:T(8,128)(2,1)S(1)} %bitcast.192, pred[128,255]{1,0:T(8,128)(4,1)S(1)} %get-tuple-element.44, f32[64,128,255]{2,1,0:T(8,128)} %reshape.132), kind=kOutput, calls=%fused_computation.1 | convolution fusion | flops 77291520 | bytes 9435008 | tf_op jit(solution)/shard_map/dot_general | solution.py:52
  91.4 5.4 %fusion.51 = f32[64,16,128]{2,1,0:T(8,128)} fusion(f32[64,16,128]{2,1,0:T(8,128)S(1)} %fusion, bf16[255,64,16]{0,2,1:T(8,128)(2,1)S(1)} %bitcast.193, pred[128,255]{1,0:T(8,128)(4,1)S(1)} %get-tuple-element.44, f32[64,128,255]{2,1,0:T(8,128)} %reshape.132), kind=kOutput, calls=%fused_computation.94 | convolution fusion | flops 71155712 | bytes 9959296 | tf_op jit(solution)/shard_map/dot_general | solution.py:51
  96.8 2.1 %copy.55 = f32[128,1024]{1,0:T(8,128)} copy(f32[128,1024]{0,1:T(8,128)} %bitcast.195) | data formatting | bytes 1048576 | tf_op jit(solution)/shard_map/reshape | solution.py:55
  98.8 7.0 %fusion.4 = f32[64,16,128]{2,1,0:T(8,128)S(1)} fusion(bf16[255,64,16]{0,2,1:T(8,128)(2,1)S(1)} %bitcast.190, pred[128,255]{1,0:T(8,128)(4,1)S(1)} %get-tuple-element.43, f32[64,128,255]{2,1,0:T(8,128)} %reshape.132), kind=kOutput, calls=%fused_computation.5 | convolution fusion | flops 77291520 | bytes 9435008 | tf_op jit(solution)/shard_map/dot_general | solution.py:52
  105.8 4.6 %fusion.48 = f32[64,16,128]{2,1,0:T(8,128)S(1)} fusion(f32[64,16,128]{2,1,0:T(8,128)S(1)} %fusion.4, bf16[255,64,16]{0,2,1:T(8,128)(2,1)S(1)} %bitcast.191, pred[128,255]{1,0:T(8,128)(4,1)S(1)} %get-tuple-element.43, f32[64,128,255]{2,1,0:T(8,128)} %reshape.132), kind=kOutput, calls=%fused_computation.93 | convolution fusion | flops 71155712 | bytes 9959296 | tf_op jit(solution)/shard_map/dot_general | solution.py:51
  111.4 1.9 %multiply_reduce_fusion = f32[256]{0:T(256)S(1)} fusion(f32[128,1024]{1,0:T(8,128)} %copy.55, f32[128,1024]{1,0:T(8,128)} %copy.54, bf16[256,1024]{1,0:T(8,128)(2,1)} %param.11, bf16[256,1024]{1,0:T(8,128)(2,1)} %param.10), kind=kLoop, calls=%fused_computation.140 | loop fusion | flops 1834752 | bytes 2098176 | tf_op jit(solution)/shard_map/reduce_sum | solution.py:129
  113.2 10.6 %all-gather.1 = f32[8,1,256]{2,1,0:T(1,128)S(1)} all-gather(f32[1,1,256]{2,1,0:T(1,128)S(1)} %bitcast.229), channel_id=2, replica_groups=mesh['ctx'=32,'tp'=8] {'tp'}, dimensions={0}, use_global_device_ids=true | all-gather | bytes 9216 | tf_op jit(solution)/shard_map/all_gather | solution.py:130
  124.3 2.6 %multiply_convert_fusion = bf16[256,1024]{1,0:T(8,128)(2,1)} fusion(f32[1024]{0:T(1024)S(1)} %copy-done.15, f32[256]{0:T(256)S(1)} %add_rsqrt_fusion, f32[128,1024]{1,0:T(8,128)} %copy.55, f32[128,1024]{1,0:T(8,128)} %copy.54, bf16[256,1024]{1,0:T(8,128)(2,1)} %param.11, bf16[256,1024]{1,0:T(8,128)(2,1)} %param.10), kind=kLoop, calls=%fused_computation.139 | loop fusion | flops 2097152 | bytes 2626560 | tf_op jit(solution)/shard_map/convert_element_type | solution.py:131
  131.7 2.1 %divide_convert_fusion = bf16[256,8,128]{2,0,1:T(8,128)(2,1)S(1)} fusion(bf16[256,8,128]{2,0,1:T(8,128)(2,1)} %collective-permute-done.5, f32[256,8,128]{2,0,1:T(8,128)} %copy-done.7, f32[256,8]{0,1:T(8,128)S(1)} %get-tuple-element.34, f32[256,8]{0,1:T(8,128)S(1)} %get-tuple-element.36, f32[256,8]{0,1:T(8,128)S(1)} %get-tuple-element.35), kind=kLoop, calls=%fused_computation.138 | loop fusion | flops 1572864 | bytes 2121728 | tf_op jit(solution)/shard_map/convert_element_type | solution.py:142
  (89 shorter events, 21.8 us)
Async XLA Ops:
  0.6 14.1 %copy-start.13 = (f32[64,128]{1,0:T(8,128)S(1)}, f32[64,128]{1,0:T(8,128)}, u32[]{:S(2)}) copy-start(f32[64,128]{1,0:T(8,128)} %param.14) | copy-start | bytes 98308
  2.8 73.1 %collective-permute-start = (bf16[127,1024]{1,0:T(8,128)(2,1)}, bf16[127,1024]{1,0:T(8,128)(2,1)S(1)}, u32[]{:S(2)}, u32[]{:S(2)}) collective-permute-start(bf16[127,1024]{1,0:T(8,128)(2,1)} %slice.176), channel_id=1, source_target_pairs={{0,8},{8,16},{16,24},{24,32},{32,40},{40,48},{48,56},{56,64},{64,7... | collective-permute-start | bytes 780296 | tf_op jit(solution)/shard_map/ppermute | solution.py:15
  6.6 40.6 %collective-permute-start.2 = (bf16[256,1024]{1,0:T(8,128)(2,1)}, bf16[256,1024]{1,0:T(8,128)(2,1)}, u32[]{:S(2)}, u32[]{:S(2)}) collective-permute-start(bf16[256,1024]{1,0:T(8,128)(2,1)} %param.16), channel_id=1, source_target_pairs={{16,0},{24,8},{32,16},{40,24},{48,32},{56,40},{64,48},{72,56},{80,... | collective-permute-start | bytes 1572872 | tf_op jit(solution)/shard_map/ppermute | solution.py:15
  10.2 30.1 %collective-permute-start.1 = (bf16[2,256,1024]{2,1,0:T(8,128)(2,1)}, bf16[2,256,1024]{2,1,0:T(8,128)(2,1)S(1)}, u32[]{:S(2)}, u32[]{:S(2)}) collective-permute-start(bf16[2,256,1024]{2,1,0:T(8,128)(2,1)} %pad_maximum_fusion), channel_id=1, source_target_pairs={{0,8},{8,16},{16,24},{24,32},{32,40},{40,48},{48,56},{56,64},{64,7... | collective-permute-start | bytes 3145736 | tf_op jit(solution)/shard_map/ppermute | solution.py:15
  24.0 16.0 %copy-start.16 = (s32[32]{0:T(128)S(1)}, s32[32]{0:T(128)}, u32[]{:S(2)}) copy-start(s32[32]{0:T(128)} %param.19) | copy-start | bytes 388
  24.0 16.5 %copy-start.1 = (bf16[256,1024]{1,0:T(8,128)(2,1)S(1)}, bf16[256,1024]{1,0:T(8,128)(2,1)}, u32[]{:S(2)}) copy-start(bf16[256,1024]{1,0:T(8,128)(2,1)} %param.17) | copy-start | bytes 1572868
  40.0 2.8 %copy-start.9 = (bf16[256,1024]{1,0:T(8,128)(2,1)S(1)}, bf16[256,1024]{1,0:T(8,128)(2,1)}, u32[]{:S(2)}) copy-start(bf16[256,1024]{1,0:T(8,128)(2,1)} %param.16) | copy-start | bytes 1572868
  40.3 4.7 %copy-start = (bf16[256,1024]{1,0:T(8,128)(2,1)S(1)}, bf16[256,1024]{1,0:T(8,128)(2,1)}, u32[]{:S(2)}) copy-start(bf16[256,1024]{1,0:T(8,128)(2,1)} %param.18) | copy-start | bytes 1572868
  45.1 13.0 %copy-start.12 = (bf16[512,128]{1,0:T(8,128)(2,1)}, bf16[512,128]{1,0:T(8,128)(2,1)S(1)}, u32[]{:S(2)}) copy-start(bf16[512,128]{1,0:T(8,128)(2,1)S(1)} %get-tuple-element.78) | copy-start | bytes 393220
  45.1 15.5 %copy-start.10 = (bf16[512,128]{1,0:T(8,128)(2,1)}, bf16[512,128]{1,0:T(8,128)(2,1)S(1)}, u32[]{:S(2)}) copy-start(bf16[512,128]{1,0:T(8,128)(2,1)S(1)} %get-tuple-element.77) | copy-start | bytes 393220
  61.0 1.1 copy-start.14
  63.4 68.3 %collective-permute-start.3 = (f32[256,8]{0,1:T(8,128)S(1)}, f32[256,8]{0,1:T(8,128)S(1)}, u32[]{:S(2)}, u32[]{:S(2)}) collective-permute-start(f32[256,8]{0,1:T(8,128)S(1)} %concatenate.30), channel_id=1, source_target_pairs={{0,16},{8,24},{16,32},{24,40},{32,48},{40,56},{48,64},{56,72},{64,... | collective-permute-start | bytes 24584 | tf_op jit(solution)/shard_map/ppermute | solution.py:15
  69.4 62.3 %collective-permute-start.4 = (f32[256,8]{0,1:T(8,128)}, f32[256,8]{0,1:T(8,128)S(1)}, u32[]{:S(2)}, u32[]{:S(2)}) collective-permute-start(f32[256,8]{0,1:T(8,128)} %concatenate.29), channel_id=1, source_target_pairs={{0,16},{8,24},{16,32},{24,40},{32,48},{40,56},{48,64},{56,72},{64,... | collective-permute-start | bytes 24584 | tf_op jit(solution)/shard_map/ppermute | solution.py:15
  78.3 53.4 %collective-permute-start.5 = (bf16[256,8,128]{2,0,1:T(8,128)(2,1)}, bf16[256,8,128]{2,0,1:T(8,128)(2,1)}, u32[]{:S(2)}, u32[]{:S(2)}) collective-permute-start(bf16[256,8,128]{2,0,1:T(8,128)(2,1)} %copy-done.14), channel_id=1, source_target_pairs={{0,16},{8,24},{16,32},{24,40},{32,48},{40,56},{48,64},{56,72},{64,... | collective-permute-start | bytes 1572872 | tf_op jit(solution)/shard_map/ppermute | solution.py:15
  110.4 13.9 %copy-start.15 = (f32[1024]{0:T(1024)S(1)}, f32[1024]{0:T(1024)}, u32[]{:S(2)}) copy-start(f32[1024]{0:T(1024)} %param.15) | copy-start | bytes 12292
  110.4 16.5 %copy-start.2 = (f32[256,512]{0,1:T(8,128)S(1)}, f32[256,512]{0,1:T(8,128)}, u32[]{:S(2)}) copy-start(f32[256,512]{0,1:T(8,128)} %get-tuple-element.64) | copy-start | bytes 1572868
  111.4 15.9 %copy-start.3 = (f32[256,512]{0,1:T(8,128)S(1)}, f32[256,512]{0,1:T(8,128)}, u32[]{:S(2)}) copy-start(f32[256,512]{0,1:T(8,128)} %get-tuple-element.66) | copy-start | bytes 1572868
  123.8 3.9 %copy-start.4 = (f32[256,512]{0,1:T(8,128)S(1)}, f32[256,512]{0,1:T(8,128)}, u32[]{:S(2)}) copy-start(f32[256,512]{0,1:T(8,128)} %get-tuple-element.68) | copy-start | bytes 1572868
  124.2 3.9 %copy-start.5 = (f32[256,512]{0,1:T(8,128)S(1)}, f32[256,512]{0,1:T(8,128)}, u32[]{:S(2)}) copy-start(f32[256,512]{0,1:T(8,128)} %get-tuple-element.70) | copy-start | bytes 1572868
  124.2 4.3 %copy-start.6 = (f32[256,512]{0,1:T(8,128)S(1)}, f32[256,512]{0,1:T(8,128)}, u32[]{:S(2)}) copy-start(f32[256,512]{0,1:T(8,128)} %get-tuple-element.72) | copy-start | bytes 1572868
  126.9 2.1 %copy-start.8 = (f32[256,512]{0,1:T(8,128)S(1)}, f32[256,512]{0,1:T(8,128)}, u32[]{:S(2)}) copy-start(f32[256,512]{0,1:T(8,128)} %get-tuple-element.76) | copy-start | bytes 1572868
  128.6 1.7 %copy-start.11 = (bf16[512,128]{1,0:T(8,128)(2,1)S(1)}, bf16[512,128]{1,0:T(8,128)(2,1)}, u32[]{:S(2)}) copy-start(bf16[512,128]{1,0:T(8,128)(2,1)} %copy-done.10) | copy-start | bytes 393220
  130.6 1.0 copy-start.7
